TPU v7x, 32 devices: a whole 2x2x4 slice. The times are simulated.
32 devices in a mesh: replica: 4 (over y, core), fsdp: 2 (over x), tensor: 4 (over z).
Axes of the slice: x: 2, y: 2, z: 4, core: 2. Of those that a mesh axis runs over, the one named last changes fastest.
Arguments:
- grad_parts: bfloat16 [4, 2, 512, 8192], P('replica', 'fsdp', 'tensor'), may hold values from -12 to 12
- inner_params: float32 [4, 512, 8192], P('replica', 'tensor', 'fsdp'), may hold values from -0.12 to 0.12
- first_moment: float32 [4, 512, 8192], P('replica', 'tensor', 'fsdp'), may hold values from -4 to 4
- second_moment: float32 [4, 512, 8192], P('replica', 'tensor', 'fsdp'), may hold values from 0.1 to 10
- outer_params: float32 [4, 512, 2048], P('replica', 'tensor', 'fsdp'), may hold values from -0.12 to 0.12
- outer_momentum: float32 [4, 512, 2048], P('replica', 'tensor', 'fsdp'), may hold values from -0.06 to 0.06
Outputs:
- next_weights: float32 [512, 8192], P('tensor')
- outer_params_out: float32 [4, 512, 2048], P('replica', 'tensor', 'fsdp')
- outer_momentum_out: float32 [4, 512, 2048], P('replica', 'tensor', 'fsdp')
- first_out: float32 [4, 512, 8192], P('replica', 'tensor', 'fsdp')
- second_out: float32 [4, 512, 8192], P('replica', 'tensor', 'fsdp')
All inputs are finite; a program needn't handle non-finite values.
Results may differ from a plain program's by a relative error of at most 0.0003.
Values may be sent and summed in bfloat16 or wider, within the bound.
No kernel may reach another device: no remote copies, remote signals or barrier semaphores. Data moves between devices by JAX's collectives and lax.ppermute only.
A program may use at most 64 MiB of HBM per device.

v0:
```python
import jax
import jax.numpy as jnp
from jax import lax
from jax.sharding import PartitionSpec as P

STEP = 100
beta_first = 0.9
beta_second = 0.95
inner_rate = 0.01
weight_decay = 0.1
epsilon = 1e-08
outer_rate = 0.7
momentum_factor = 0.9


def inner_adamw(gradient, params, first_in, second_in):
    first_out = beta_first * first_in + (1.0 - beta_first) * gradient
    second_out = beta_second * second_in + (1.0 - beta_second) * gradient * gradient
    first_scale = 1.0 / (1.0 - beta_first**STEP)
    second_scale = 1.0 / (1.0 - beta_second**STEP)
    direction = first_out * first_scale / (jnp.sqrt(second_out * second_scale) + epsilon)
    updated = params - inner_rate * (direction + weight_decay * params)
    return (first_out, second_out, updated)


def nesterov(mean_params, outer_in, momentum):
    pseudo_grad = outer_in - mean_params
    momentum_new = momentum_factor * momentum + pseudo_grad
    params_new = outer_in - outer_rate * (pseudo_grad + momentum_factor * momentum_new)
    return (params_new, momentum_new)


def local(grad_parts, inner_params, first_moment, second_moment, outer_params, outer_momentum):
    replicas = lax.axis_size("replica")
    gradient = lax.psum_scatter(
        grad_parts[0, 0].astype(jnp.float32), "fsdp", scatter_dimension=1, tiled=True
    )
    first_out, second_out, updated = inner_adamw(
        gradient, inner_params[0], first_moment[0], second_moment[0]
    )
    share_cols = outer_params.shape[2]
    totals = lax.psum_scatter(updated, "replica", scatter_dimension=1, tiled=True)
    params_new, momentum_new = nesterov(totals / replicas, outer_params[0], outer_momentum[0])
    pieces = lax.all_gather(params_new[None], ("replica", "fsdp"), axis=0, tiled=True)
    fsdp_count = lax.axis_size("fsdp")
    row_count = params_new.shape[0]
    arranged = pieces.reshape(replicas, fsdp_count, row_count, share_cols).transpose(2, 1, 0, 3)
    next_weights = arranged.reshape(row_count, fsdp_count * replicas * share_cols)
    return (next_weights, params_new[None], momentum_new[None], first_out[None], second_out[None])


def solution(mesh):
    return jax.shard_map(
        local,
        mesh=mesh,
        in_specs=(
            P("replica", "fsdp", "tensor", None),
            P("replica", "tensor", "fsdp"),
            P("replica", "tensor", "fsdp"),
            P("replica", "tensor", "fsdp"),
            P("replica", "tensor", "fsdp"),
            P("replica", "tensor", "fsdp"),
        ),
        out_specs=(
            P("tensor", None),
            P("replica", "tensor", "fsdp"),
            P("replica", "tensor", "fsdp"),
            P("replica", "tensor", "fsdp"),
            P("replica", "tensor", "fsdp"),
        ),
        check_vma=False,
    )
```

profile of v0, /device:TPU:0, one launch (start us, length us, event | category | flops | bytes accessed | tf_op | source)
XLA Modules:
  0.0 165.5 jit_solution(11605220158875495596)
XLA Ops:
  7.2 0.0 reduce-scatter.3.cloned.1.call-start
  7.2 4.0 %bitcast_convert_fusion = f32[128,8192]{1,0:T(8,128)} fusion(bf16[1,1,128,8192]{3,2,1,0:T(8,128)(2,1)} %param.6), kind=kLoop, calls=%fused_computation.2 | loop fusion | flops 1048576 | bytes 6291456 | tf_op jit(solution)/shard_map/convert_element_type | solution.py:36
  11.2 0.0 copy-start
  11.2 0.0 reduce-scatter.3.cloned.1.call-update
  11.3 0.0 reduce-scatter.5.cloned.1.call-start
  11.3 57.2 %reduce-scatter.3.cloned.1.call-done = f32[128,4096]{1,0:T(8,128)} async-done(((f32[128,8192]{1,0:T(8,128)}), f32[128,4096]{1,0:T(8,128)}) %reduce-scatter.3.cloned.1.call-update) | async-done | bytes 2097168 | tf_op jit(solution)/shard_map/reduce_scatter | solution.py:35
  68.5 0.0 copy-done
  68.5 7.1 %fusion.4 = (f32[1,128,4096]{2,1,0:T(8,128)}, f32[128,4096]{1,0:T(8,128)}, f32[1,128,4096]{2,1,0:T(8,128)}) fusion(f32[128,4096]{1,0:T(8,128)} %reduce-scatter.3.cloned.1.call-done, f32[1,128,4096]{2,1,0:T(8,128)S(1)} %copy-done, f32[1,128,4096]{2,1,0:T(8,128)} %param.8, f32[1,128,4096]{2,1,0:T(8,128)} %param.7), kind=kLoop, calls=%fused_computation.9 | loop fusion | flops 7864320 | bytes 14680064 | tf_op jit(solution)/shard_map/broadcast_in_dim | solution.py:49
  75.6 0.0 copy-start.1
  75.7 0.0 copy-start.2
  75.7 0.0 reduce-scatter.5.cloned.1.call-update
  75.7 0.0 all-gather.3.cloned.1.call-start
  75.7 31.3 %reduce-scatter.5.cloned.1.call-done = f32[128,1024]{1,0:T(8,128)} async-done(((f32[128,4096]{1,0:T(8,128)}), f32[128,1024]{1,0:T(8,128)}) %reduce-scatter.5.cloned.1.call-update) | async-done | bytes 524304 | tf_op jit(solution)/shard_map/reduce_scatter | solution.py:42
  107.0 0.0 copy-done.1
  107.0 0.0 copy-done.2
  107.0 2.2 %fusion.5 = (f32[1,128,1024]{2,1,0:T(8,128)}, f32[128,1024]{1,0:T(8,128)}) fusion(f32[128,1024]{1,0:T(8,128)} %reduce-scatter.5.cloned.1.call-done, f32[1,128,1024]{2,1,0:T(8,128)S(1)} %copy-done.1, f32[1,128,1024]{2,1,0:T(8,128)S(1)} %copy-done.2), kind=kLoop, calls=%fused_computation.13 | loop fusion | flops 1048576 | bytes 2621440 | tf_op jit(solution)/shard_map/broadcast_in_dim | solution.py:49
  109.2 0.0 all-gather.3.cloned.1.call-update
  109.2 36.9 %all-gather.3.cloned.1.call-done = f32[1024,1024]{1,0:T(8,128)} async-done(((f32[128,1024]{1,0:T(8,128)}), f32[1024,1024]{1,0:T(8,128)}) %all-gather.3.cloned.1.call-update) | async-done | bytes 4194320 | tf_op jit(solution)/shard_map/all_gather | solution.py:44
  146.1 6.9 %copy.11 = f32[128,2,4,1024]{3,2,1,0:T(4,128)} copy(f32[128,2,4,1024]{3,0,1,2:T(8,128)} %bitcast.51) | data formatting | bytes 8388608 | tf_op jit(solution)/shard_map/transpose | solution.py:47
  153.0 6.0 %reshape.25 = f32[128,8192]{1,0:T(8,128)} reshape(f32[128,2,4,1024]{3,2,1,0:T(4,128)} %copy.11) | data formatting | bytes 8388608 | tf_op jit(solution)/shard_map/reshape | solution.py:48
Async XLA Ops:
  7.2 61.4 %reduce-scatter.3.cloned.1.call-start = ((), (), s32[]{:S(2)}) async-start(), calls=%async_computation.2 | async-start | bytes 6291456 | tf_op jit(solution)/shard_map/reduce_scatter | solution.py:35
  11.2 57.3 %copy-start = (f32[1,128,4096]{2,1,0:T(8,128)S(1)}, f32[1,128,4096]{2,1,0:T(8,128)}, u32[]{:S(2)}) copy-start(f32[1,128,4096]{2,1,0:T(8,128)} %param.9) | copy-start | bytes 6291460
  11.3 95.8 %reduce-scatter.5.cloned.1.call-start = ((), (), s32[]{:S(2)}) async-start(), calls=%async_computation.3 | async-start | bytes 2621440 | tf_op jit(solution)/shard_map/reduce_scatter | solution.py:42
  75.6 31.4 %copy-start.1 = (f32[1,128,1024]{2,1,0:T(8,128)S(1)}, f32[1,128,1024]{2,1,0:T(8,128)}, u32[]{:S(2)}) copy-start(f32[1,128,1024]{2,1,0:T(8,128)} %param.10) | copy-start | bytes 1572868
  75.7 31.4 %copy-start.2 = (f32[1,128,1024]{2,1,0:T(8,128)S(1)}, f32[1,128,1024]{2,1,0:T(8,128)}, u32[]{:S(2)}) copy-start(f32[1,128,1024]{2,1,0:T(8,128)} %param.11) | copy-start | bytes 1572868
  75.7 70.4 %all-gather.3.cloned.1.call-start = ((), (), s32[]{:S(2)}) async-start(), calls=%async_computation.4 | async-start | bytes 4718592 | tf_op jit(solution)/shard_map/all_gather | solution.py:44
Sparse Core Ops, SparseCore 0:
  11.4 57.0 reduce-scatter.2
  75.8 31.1 reduce-scatter.4
  109.5 36.5 all-gather.2
where the time goes:
time: 166 us
  waiting for transfers between devices  125 us (75%)
  between operations  13.7 us (8%)
  other arithmetic  13.3 us (8%)
  local copies, waits for them, and re-layouts  12.9 us (8%)
    reduce_scatter x1, waiting for transfers between devices, local(): lax.psum_scatter(grad_parts[0, 0].astype(jnp.float32), 'fsdp', scatter_di...  57.2 us
    all_gather x1, waiting for transfers between devices, local(): lax.all_gather(params_new[None], ('replica', 'fsdp'), axis=0, tiled=True)  36.9 us
    reduce_scatter x1, waiting for transfers between devices, local(): lax.psum_scatter(updated, 'replica', scatter_dimension=1, tiled=True)  31.3 us
    broadcast_in_dim x1, other arithmetic, local(): second_out[None]  7.13 us
    transpose x1, local copies, waits for them, and re-layouts, local(): pieces.reshape(replicas, fsdp_count, row_count, share_cols)  6.86 us
    reshape x1, local copies, waits for them, and re-layouts, local(): arranged.reshape(row_count, fsdp_count * replicas * share_cols)  6.05 us
    convert_element_type x1, other arithmetic, local(): grad_parts[0, 0].astype(jnp.float32)  4.03 us
  transfers between devices with their start and end apart: 3, of which 3 were waited for; matrix products, arithmetic and copies ran while one was open for 0% of the time, Pallas kernels for 0%

commit v1 on v0

--- a/solution.py
+++ b/solution.py
@@ -1,3 +1,4 @@
+import functools
 import jax
 import jax.numpy as jnp
 from jax import lax
@@ -11,6 +12,35 @@
 epsilon = 1e-08
 outer_rate = 0.7
 momentum_factor = 0.9
+
+
+def name_matrix(field, mesh_name):
+    state_now, everything, v1 = (
+        jax.lax.axis_size(mesh_name),
+        jax.lax.axis_index(mesh_name),
+        field.shape[0],
+    )
+    by_rank = [dev * state_now if d == 0 else dev for d, dev in enumerate(field.shape)]
+    z2 = lax.dynamic_update_slice_in_dim(
+        jnp.zeros(by_rank, field.dtype), field, everything * v1, axis=0
+    )
+    y_new = raw_out = field
+    for at in tuple(range(1, state_now // 2 + 1)):
+        y_new = jax.lax.ppermute(
+            y_new, mesh_name, [(d, (d + 1) % state_now) for d in range(state_now)]
+        )
+        z2 = lax.dynamic_update_slice_in_dim(z2, y_new, (everything - at) % state_now * v1, axis=0)
+        if 2 * at < state_now:
+            raw_out = jax.lax.ppermute(
+                raw_out, mesh_name, [(d, (d - 1) % state_now) for d in range(state_now)]
+            )
+            z2 = lax.dynamic_update_slice_in_dim(
+                z2, raw_out, (everything + at) % state_now * v1, axis=0
+            )
+    return z2
+
+
+extend_the_figure = functools.partial(name_matrix, mesh_name=("replica", "fsdp"))
 
 
 def inner_adamw(gradient, params, first_in, second_in):
@@ -41,7 +71,7 @@
     share_cols = outer_params.shape[2]
     totals = lax.psum_scatter(updated, "replica", scatter_dimension=1, tiled=True)
     params_new, momentum_new = nesterov(totals / replicas, outer_params[0], outer_momentum[0])
-    pieces = lax.all_gather(params_new[None], ("replica", "fsdp"), axis=0, tiled=True)
+    pieces = extend_the_figure(params_new[None])
     fsdp_count = lax.axis_size("fsdp")
     row_count = params_new.shape[0]
     arranged = pieces.reshape(replicas, fsdp_count, row_count, share_cols).transpose(2, 1, 0, 3)

time: 166 us -> 211 us (1.27)
  waiting for transfers between devices: 125 us -> 153 us
  starting transfers between devices: 0.12 us -> 10.8 us
  local copies, waits for them, and re-layouts: 12.9 us -> 20.4 us
    ppermute x0 -> x7, waiting for transfers between devices: none -> 64 us  [the longest x4 41.7 us: name_matrix(): jax.lax.ppermute(y_new, mesh_name, [(d, (d + 1) % state_now) for d in ran...]
    all_gather x1 -> x0, waiting for transfers between devices: 36.9 us -> none  [local(): lax.all_gather(params_new[None], ('replica', 'fsdp'), axis=0, tiled=True)]
    ppermute x0 -> x7, starting transfers between devices: none -> 10.7 us  [the longest x3 5.88 us: name_matrix(): jax.lax.ppermute(raw_out, mesh_name, [(d, (d - 1) % state_now) for d in r...]
    dynamic_update_slice x0 -> x7, local copies, waits for them, and re-layouts: none -> 6.87 us  [the longest x4 4.39 us: name_matrix(): lax.dynamic_update_slice_in_dim(z2, y_new, (everything - at) % state_now...]
    reshape x1 -> x0, local copies, waits for them, and re-layouts: 6.05 us -> none  [local(): arranged.reshape(row_count, fsdp_count * replicas * share_cols)]
    unnamed x6 -> x15, local copies, waits for them, and re-layouts: 0.01 us -> 5.62 us
    broadcast_in_dim x0 -> x1, local copies, waits for them, and re-layouts: none -> 2.54 us  [name_matrix(): jnp.zeros(by_rank, field.dtype)]
  transfers between devices with their start and end apart: 3 -> 9, of which waited for: 3 -> 9; matrix products, arithmetic and copies ran while one was open for 0% -> 3% of each run, Pallas kernels for 0% -> 0%
where the time goes in v1:
time: 211 us
  waiting for transfers between devices  153 us (73%)
  local copies, waits for them, and re-layouts  20.4 us (10%)
  between operations  14.1 us (7%)
  other arithmetic  13 us (6%)
  starting transfers between devices  10.8 us (5%)
    reduce_scatter x1, waiting for transfers between devices, local(): lax.psum_scatter(grad_parts[0, 0].astype(jnp.float32), 'fsdp', scatter_di...  57.2 us
    ppermute x4, waiting for transfers between devices, name_matrix(): jax.lax.ppermute(y_new, mesh_name, [(d, (d + 1) % state_now) for d in ran...  41.7 us
    reduce_scatter x1, waiting for transfers between devices, local(): lax.psum_scatter(updated, 'replica', scatter_dimension=1, tiled=True)  31.3 us
    ppermute x3, waiting for transfers between devices, name_matrix(): jax.lax.ppermute(raw_out, mesh_name, [(d, (d - 1) % state_now) for d in r...  22.2 us
    broadcast_in_dim x1, other arithmetic, local(): second_out[None]  7.13 us
    ppermute x3, starting transfers between devices, name_matrix(): jax.lax.ppermute(raw_out, mesh_name, [(d, (d - 1) % state_now) for d in r...  5.88 us
    unnamed x15, local copies, waits for them, and re-layouts  5.62 us
    transpose x1, local copies, waits for them, and re-layouts, local(): pieces.reshape(replicas, fsdp_count, row_count, share_cols)  5.33 us
  transfers between devices with their start and end apart: 9, of which 9 were waited for; matrix products, arithmetic and copies ran while one was open for 3% of the time, Pallas kernels for 0%

profile of v1, /device:TPU:0, one launch (start us, length us, event | category | flops | bytes accessed | tf_op | source)
XLA Modules:
  0.0 210.8 jit_solution(9360150527827884832)
XLA Ops:
  7.2 0.0 reduce-scatter.3.cloned.1.call-start
  7.2 4.0 %bitcast_convert_fusion = f32[128,8192]{1,0:T(8,128)} fusion(bf16[1,1,128,8192]{3,2,1,0:T(8,128)(2,1)} %param.6), kind=kLoop, calls=%fused_computation.2 | loop fusion | flops 1048576 | bytes 6291456 | tf_op jit(solution)/shard_map/convert_element_type | solution.py:66
  11.2 0.0 copy-start
  11.2 0.0 reduce-scatter.3.cloned.1.call-update
  11.3 0.0 reduce-scatter.5.cloned.1.call-start
  11.3 57.2 %reduce-scatter.3.cloned.1.call-done = f32[128,4096]{1,0:T(8,128)} async-done(((f32[128,8192]{1,0:T(8,128)}), f32[128,4096]{1,0:T(8,128)}) %reduce-scatter.3.cloned.1.call-update) | async-done | bytes 2097168 | tf_op jit(solution)/shard_map/reduce_scatter | solution.py:65
  68.5 0.0 copy-done
  68.5 7.1 %fusion.4 = (f32[1,128,4096]{2,1,0:T(8,128)}, f32[128,4096]{1,0:T(8,128)}, f32[1,128,4096]{2,1,0:T(8,128)}) fusion(f32[128,4096]{1,0:T(8,128)} %reduce-scatter.3.cloned.1.call-done, f32[1,128,4096]{2,1,0:T(8,128)S(1)} %copy-done, f32[1,128,4096]{2,1,0:T(8,128)} %param.8, f32[1,128,4096]{2,1,0:T(8,128)} %param.7), kind=kLoop, calls=%fused_computation.9 | loop fusion | flops 7864320 | bytes 14680064 | tf_op jit(solution)/shard_map/broadcast_in_dim | solution.py:79
  75.6 0.0 reduce-scatter.5.cloned.1.call-update
  75.7 0.0 copy-start.1
  75.7 0.0 copy-start.2
  75.7 31.3 %reduce-scatter.5.cloned.1.call-done = f32[128,1024]{1,0:T(8,128)} async-done(((f32[128,4096]{1,0:T(8,128)}), f32[128,1024]{1,0:T(8,128)}) %reduce-scatter.5.cloned.1.call-update) | async-done | bytes 524304 | tf_op jit(solution)/shard_map/reduce_scatter | solution.py:72
  107.0 0.0 copy-start.3
  107.0 2.5 %broadcast_in_dim.16 = f32[8,128,1024]{2,1,0:T(8,128)} broadcast(f32[]{:T(128)} %constant.63.clone.1), dimensions={} | broadcast | bytes 4194308 | tf_op jit(solution)/shard_map/broadcast_in_dim | solution.py:25
  109.6 0.0 copy-done.1
  109.6 0.0 copy-done.2
  109.6 0.0 copy-done.3
  109.6 1.0 constant_dynamic-update-slice_fusion.7
  110.6 0.0 copy-start.6
  110.6 1.5 collective-permute-start
  112.0 1.2 collective-permute-start.1
  113.2 12.5 %collective-permute-done = f32[1,128,1024]{2,1,0:T(8,128)S(1)} collective-permute-done((f32[1,128,1024]{2,1,0:T(8,128)S(1)}, f32[1,128,1024]{2,1,0:T(8,128)S(1)}, u32[]{:S(2)}, u32[]{:S(2)}) %collective-permute-start) | collective-permute-done | bytes 524320 | tf_op jit(solution)/shard_map/ppermute | solution.py:29
  125.7 0.0 copy-start.4
  125.7 1.1 collective-permute-start.2
  126.8 9.2 %collective-permute-done.1 = f32[1,128,1024]{2,1,0:T(8,128)S(1)} collective-permute-done((f32[1,128,1024]{2,1,0:T(8,128)S(1)}, f32[1,128,1024]{2,1,0:T(8,128)S(1)}, u32[]{:S(2)}, u32[]{:S(2)}) %collective-permute-start.1) | collective-permute-done | bytes 524320 | tf_op jit(solution)/shard_map/ppermute | solution.py:34
  136.0 2.3 %collective-permute-start.3 = (f32[1,128,1024]{2,1,0:T(8,128)S(1)}, f32[1,128,1024]{2,1,0:T(8,128)S(1)}, u32[]{:S(2)}, u32[]{:S(2)}) collective-permute-start(f32[1,128,1024]{2,1,0:T(8,128)S(1)} %collective-permute-done.1), channel_id=1, source_target_pairs={{0,28},{4,0},{8,4},{12,8},{16,12},{20,16},{24,20},{28,24},{1,29},{... | collective-permute-start | bytes 1572872 | tf_op jit(solution)/shard_map/ppermute | solution.py:34
  138.4 0.0 copy-done.4
  138.4 9.9 %collective-permute-done.2 = f32[1,128,1024]{2,1,0:T(8,128)} collective-permute-done((f32[1,128,1024]{2,1,0:T(8,128)S(1)}, f32[1,128,1024]{2,1,0:T(8,128)}, u32[]{:S(2)}, u32[]{:S(2)}) %collective-permute-start.2) | collective-permute-done | bytes 524320 | tf_op jit(solution)/shard_map/ppermute | solution.py:29
  148.3 0.0 copy-done.6
  148.3 1.1 collective-permute-start.4
  149.4 0.0 copy-start.5
  149.4 0.9 fusion.6
  150.3 8.2 %collective-permute-done.3 = f32[1,128,1024]{2,1,0:T(8,128)S(1)} collective-permute-done((f32[1,128,1024]{2,1,0:T(8,128)S(1)}, f32[1,128,1024]{2,1,0:T(8,128)S(1)}, u32[]{:S(2)}, u32[]{:S(2)}) %collective-permute-start.3) | collective-permute-done | bytes 524320 | tf_op jit(solution)/shard_map/ppermute | solution.py:34
  158.5 2.3 %collective-permute-start.5 = (f32[1,128,1024]{2,1,0:T(8,128)S(1)}, f32[1,128,1024]{2,1,0:T(8,128)S(1)}, u32[]{:S(2)}, u32[]{:S(2)}) collective-permute-start(f32[1,128,1024]{2,1,0:T(8,128)S(1)} %collective-permute-done.3), channel_id=1, source_target_pairs={{0,28},{4,0},{8,4},{12,8},{16,12},{20,16},{24,20},{28,24},{1,29},{... | collective-permute-start | bytes 1572872 | tf_op jit(solution)/shard_map/ppermute | solution.py:34
  160.9 0.0 copy-done.5
  160.9 0.8 constant_dynamic-update-slice_fusion.6
  161.7 8.9 %collective-permute-done.4 = f32[1,128,1024]{2,1,0:T(8,128)S(1)} collective-permute-done((f32[1,128,1024]{2,1,0:T(8,128)}, f32[1,128,1024]{2,1,0:T(8,128)S(1)}, u32[]{:S(2)}, u32[]{:S(2)}) %collective-permute-start.4) | collective-permute-done | bytes 524320 | tf_op jit(solution)/shard_map/ppermute | solution.py:29
  170.6 1.1 collective-permute-start.6
  171.8 0.8 constant_dynamic-update-slice_fusion.5
  172.6 1.9 constant_dynamic-update-slice_fusion.4
  174.5 0.8 constant_dynamic-update-slice_fusion.3
  175.3 0.8 constant_dynamic-update-slice_fusion.2
  176.1 4.8 %collective-permute-done.5 = f32[1,128,1024]{2,1,0:T(8,128)S(1)} collective-permute-done((f32[1,128,1024]{2,1,0:T(8,128)S(1)}, f32[1,128,1024]{2,1,0:T(8,128)S(1)}, u32[]{:S(2)}, u32[]{:S(2)}) %collective-permute-start.5) | collective-permute-done | bytes 524320 | tf_op jit(solution)/shard_map/ppermute | solution.py:34
  181.0 0.8 constant_dynamic-update-slice_fusion.1
  181.8 10.4 %collective-permute-done.6 = f32[1,128,1024]{2,1,0:T(8,128)S(1)} collective-permute-done((f32[1,128,1024]{2,1,0:T(8,128)S(1)}, f32[1,128,1024]{2,1,0:T(8,128)S(1)}, u32[]{:S(2)}, u32[]{:S(2)}) %collective-permute-start.6) | collective-permute-done | bytes 524320 | tf_op jit(solution)/shard_map/ppermute | solution.py:29
  192.2 0.8 constant_dynamic-update-slice_fusion
  193.0 5.3 %copy.11 = f32[128,2,4,1024]{0,3,2,1:T(8,128)} copy(f32[128,2,4,1024]{3,0,1,2:T(8,128)} %bitcast.8) | data formatting | bytes 8388608 | tf_op jit(solution)/shard_map/transpose | solution.py:77
  198.4 5.6 %copy.12 = f32[128,8192]{1,0:T(8,128)} copy(f32[128,8192]{0,1:T(8,128)} %bitcast.58) | data formatting | bytes 8388608
Async XLA Ops:
  7.2 61.4 %reduce-scatter.3.cloned.1.call-start = ((), (), s32[]{:S(2)}) async-start(), calls=%async_computation.2 | async-start | bytes 6291456 | tf_op jit(solution)/shard_map/reduce_scatter | solution.py:65
  11.2 57.3 %copy-start = (f32[1,128,4096]{2,1,0:T(8,128)S(1)}, f32[1,128,4096]{2,1,0:T(8,128)}, u32[]{:S(2)}) copy-start(f32[1,128,4096]{2,1,0:T(8,128)} %param.9) | copy-start | bytes 6291460
  11.3 95.8 %reduce-scatter.5.cloned.1.call-start = ((), (), s32[]{:S(2)}) async-start(), calls=%async_computation.3 | async-start | bytes 2621440 | tf_op jit(solution)/shard_map/reduce_scatter | solution.py:72
  75.7 33.9 %copy-start.1 = (f32[1,128,1024]{2,1,0:T(8,128)S(1)}, f32[1,128,1024]{2,1,0:T(8,128)}, u32[]{:S(2)}) copy-start(f32[1,128,1024]{2,1,0:T(8,128)} %param.11) | copy-start | bytes 1572868
  75.7 33.9 %copy-start.2 = (f32[1,128,1024]{2,1,0:T(8,128)S(1)}, f32[1,128,1024]{2,1,0:T(8,128)}, u32[]{:S(2)}) copy-start(f32[1,128,1024]{2,1,0:T(8,128)} %param.10) | copy-start | bytes 1572868
  107.0 2.5 %copy-start.3 = (f32[128,1024]{1,0:T(8,128)S(1)}, f32[128,1024]{1,0:T(8,128)}, u32[]{:S(2)}) copy-start(f32[128,1024]{1,0:T(8,128)} %reduce-scatter.5.cloned.1.call-done) | copy-start | bytes 1572868
  110.6 37.7 %copy-start.6 = (f32[1,128,1024]{2,1,0:T(8,128)}, f32[1,128,1024]{2,1,0:T(8,128)S(1)}, u32[]{:S(2)}) copy-start(f32[1,128,1024]{2,1,0:T(8,128)S(1)} %get-tuple-element.11) | copy-start | bytes 1572868
  110.6 15.1 %collective-permute-start = (f32[1,128,1024]{2,1,0:T(8,128)S(1)}, f32[1,128,1024]{2,1,0:T(8,128)S(1)}, u32[]{:S(2)}, u32[]{:S(2)}) collective-permute-start(f32[1,128,1024]{2,1,0:T(8,128)S(1)} %get-tuple-element.11), channel_id=1, source_target_pairs={{0,4},{4,8},{8,12},{12,16},{16,20},{20,24},{24,28},{28,0},{1,5},{5... | collective-permute-start | bytes 1572872 | tf_op jit(solution)/shard_map/ppermute | solution.py:29
  112.0 24.0 %collective-permute-start.1 = (f32[1,128,1024]{2,1,0:T(8,128)S(1)}, f32[1,128,1024]{2,1,0:T(8,128)S(1)}, u32[]{:S(2)}, u32[]{:S(2)}) collective-permute-start(f32[1,128,1024]{2,1,0:T(8,128)S(1)} %get-tuple-element.11), channel_id=1, source_target_pairs={{0,28},{4,0},{8,4},{12,8},{16,12},{20,16},{24,20},{28,24},{1,29},{... | collective-permute-start | bytes 1572872 | tf_op jit(solution)/shard_map/ppermute | solution.py:34
  125.7 12.7 %copy-start.4 = (f32[1,128,1024]{2,1,0:T(8,128)}, f32[1,128,1024]{2,1,0:T(8,128)S(1)}, u32[]{:S(2)}) copy-start(f32[1,128,1024]{2,1,0:T(8,128)S(1)} %collective-permute-done) | copy-start | bytes 1572868
  125.7 22.6 %collective-permute-start.2 = (f32[1,128,1024]{2,1,0:T(8,128)S(1)}, f32[1,128,1024]{2,1,0:T(8,128)}, u32[]{:S(2)}, u32[]{:S(2)}) collective-permute-start(f32[1,128,1024]{2,1,0:T(8,128)S(1)} %collective-permute-done), channel_id=1, source_target_pairs={{0,4},{4,8},{8,12},{12,16},{16,20},{20,24},{24,28},{28,0},{1,5},{5... | collective-permute-start | bytes 1572872 | tf_op jit(solution)/shard_map/ppermute | solution.py:29
  136.0 22.5 %collective-permute-start.3 = (f32[1,128,1024]{2,1,0:T(8,128)S(1)}, f32[1,128,1024]{2,1,0:T(8,128)S(1)}, u32[]{:S(2)}, u32[]{:S(2)}) collective-permute-start(f32[1,128,1024]{2,1,0:T(8,128)S(1)} %collective-permute-done.1), channel_id=1, source_target_pairs={{0,28},{4,0},{8,4},{12,8},{16,12},{20,16},{24,20},{28,24},{1,29},{... | collective-permute-start | bytes 1572872 | tf_op jit(solution)/shard_map/ppermute | solution.py:34
  148.3 22.4 %collective-permute-start.4 = (f32[1,128,1024]{2,1,0:T(8,128)}, f32[1,128,1024]{2,1,0:T(8,128)S(1)}, u32[]{:S(2)}, u32[]{:S(2)}) collective-permute-start(f32[1,128,1024]{2,1,0:T(8,128)} %collective-permute-done.2), channel_id=1, source_target_pairs={{0,4},{4,8},{8,12},{12,16},{16,20},{20,24},{24,28},{28,0},{1,5},{5... | collective-permute-start | bytes 1572872 | tf_op jit(solution)/shard_map/ppermute | solution.py:29
  149.4 11.5 %copy-start.5 = (f32[1,128,1024]{2,1,0:T(8,128)S(1)}, f32[1,128,1024]{2,1,0:T(8,128)}, u32[]{:S(2)}) copy-start(f32[1,128,1024]{2,1,0:T(8,128)} %copy-done.4) | copy-start | bytes 1572868
  158.5 22.5 %collective-permute-start.5 = (f32[1,128,1024]{2,1,0:T(8,128)S(1)}, f32[1,128,1024]{2,1,0:T(8,128)S(1)}, u32[]{:S(2)}, u32[]{:S(2)}) collective-permute-start(f32[1,128,1024]{2,1,0:T(8,128)S(1)} %collective-permute-done.3), channel_id=1, source_target_pairs={{0,28},{4,0},{8,4},{12,8},{16,12},{20,16},{24,20},{28,24},{1,29},{... | collective-permute-start | bytes 1572872 | tf_op jit(solution)/shard_map/ppermute | solution.py:34
  170.6 21.6 %collective-permute-start.6 = (f32[1,128,1024]{2,1,0:T(8,128)S(1)}, f32[1,128,1024]{2,1,0:T(8,128)S(1)}, u32[]{:S(2)}, u32[]{:S(2)}) collective-permute-start(f32[1,128,1024]{2,1,0:T(8,128)S(1)} %collective-permute-done.4), channel_id=1, source_target_pairs={{0,4},{4,8},{8,12},{12,16},{16,20},{20,24},{24,28},{28,0},{1,5},{5... | collective-permute-start | bytes 1572872 | tf_op jit(solution)/shard_map/ppermute | solution.py:29
Sparse Core Ops, SparseCore 0:
  11.4 57.0 reduce-scatter.2
  75.8 31.1 reduce-scatter.4
